TPU v7x, 256 devices: a whole 4x4x8 slice. The times are simulated.
256 devices in a mesh: req: 8 (over z), seq: 32 (over y, x, core).
Axes of the slice: x: 4, y: 4, z: 8, core: 2. Of those that a mesh axis runs over, the one named last changes fastest.
Arguments:
- hidden_in: bfloat16 [16, 1024, 2048], P('req', 'seq'), may hold values from -6 to 6
- norm_gain: float32 [2048], replicated, may hold values from 0.1 to 1.9
- w_query: bfloat16 [2048, 1024], P(('req', 'seq')), may hold values from -0.125 to 0.125
- w_key: bfloat16 [2048, 512], P(('req', 'seq')), may hold values from -0.3125 to 0.3125
- w_value: bfloat16 [2048, 512], P(('req', 'seq')), may hold values from -0.125 to 0.125
- cache_keys: bfloat16 [16, 8192, 512], P('req', 'seq'), may hold values from -525 to 525
- cache_values: bfloat16 [16, 8192, 512], P('req', 'seq'), may hold values from -6 to 6
- cache_lengths: int32 [16], P('req'), may hold values from 1 to 8192, as said below
Outputs:
- attended: bfloat16 [16, 1024, 1024], P('req', 'seq')
- new_keys: bfloat16 [16, 1024, 512], P('req', 'seq')
- new_values: bfloat16 [16, 1024, 512], P('req', 'seq')
Inputs may be any that keep to these rules, and one draw needn't show every extreme that they name: `cache_lengths`: some request's cache holds exactly 8192 positions.
All inputs are finite; a program needn't handle non-finite values.
Results may differ from a plain program's by a relative error of at most 0.034.
Values may be sent and summed in bfloat16 or wider, within the bound.
No kernel may reach another device: no remote copies, remote signals or barrier semaphores. Data moves between devices by JAX's collectives and lax.ppermute only.
A program may use at most 128 MiB of HBM per device.

v0:
```python
import jax
import jax.numpy as jnp
from jax import lax
from jax.sharding import PartitionSpec as P

HEADS = 4
KV_HEADS = 2
HEAD = 256
EPSILON = 1e-06
THETA = 1000042.0
MASKED = -1e30


def tables(positions, head_size):
    half_size = head_size // 2
    frequency = THETA ** (-(jnp.arange(half_size, dtype=jnp.float32) * 2.0 / head_size))
    angles = positions.astype(jnp.float32)[..., None] * frequency
    return (jnp.cos(angles)[..., None, :], jnp.sin(angles)[..., None, :])


def rotate(values, cosine, sine_part):
    half_size = values.shape[-1] // 2
    first_half = values[..., :half_size]
    second_half = values[..., half_size:]
    return jnp.concatenate(
        [
            first_half * cosine - second_half * sine_part,
            second_half * cosine + first_half * sine_part,
        ],
        axis=-1,
    )


def attend(query_rows, key_rows, value_rows, live):
    span_len = query_rows.shape[0]
    group_size = HEADS // KV_HEADS
    query_view = query_rows.reshape(span_len, KV_HEADS, group_size, HEAD)
    key_view = key_rows.reshape(key_rows.shape[0], KV_HEADS, HEAD)
    value_view = value_rows.reshape(value_rows.shape[0], KV_HEADS, HEAD)
    scores = jnp.einsum(
        "cgeh,kgh->cgek", query_view, key_view, preferred_element_type=jnp.float32
    ) * HEAD ** (-0.5)
    mask_view = live[:, None, None, :]
    scores = jnp.where(mask_view, scores, MASKED)
    block_max = jnp.max(scores, axis=-1)
    weights = jnp.where(mask_view, jnp.exp(scores - block_max[..., None]), 0.0)
    block_sum = jnp.sum(weights, axis=-1)
    block_out = jnp.einsum(
        "cgek,kgh->cgeh",
        weights.astype(jnp.bfloat16),
        value_view,
        preferred_element_type=jnp.float32,
    )
    return (
        block_max.reshape(span_len, HEADS),
        block_sum.reshape(span_len, HEADS),
        block_out.reshape(span_len, HEADS * HEAD).astype(jnp.bfloat16),
    )


def attend_rows(query_rows, key_rows, value_rows, live):
    total_rows = query_rows.shape[0]
    row_block = min(512, total_rows)
    pieces = []
    for begin in range(0, total_rows, row_block):
        pieces.append(
            attend(
                query_rows[begin : begin + row_block],
                key_rows,
                value_rows,
                live[begin : begin + row_block],
            )
        )
    return tuple((jnp.concatenate([piece[slot] for piece in pieces], axis=0) for slot in range(3)))


def body(hidden_in, norm_gain, w_query, w_key, w_value, cache_keys, cache_values, cache_lengths):
    seq_count = lax.axis_size("seq")
    seq_seat = lax.axis_index("seq")
    req_local, slice_len, model_width = hidden_in.shape
    cache_len_dev = cache_keys.shape[1]
    span_len = slice_len * seq_count
    inputs = hidden_in.astype(jnp.float32)
    normed = (
        inputs * lax.rsqrt(jnp.mean(inputs * inputs, axis=-1, keepdims=True) + EPSILON) * norm_gain
    ).astype(jnp.bfloat16)
    flat_rows = normed.reshape(req_local * slice_len, model_width)
    full_query, full_key, full_value = (
        lax.all_gather(w_query, ("req", "seq"), axis=0, tiled=True),
        lax.all_gather(w_key, ("req", "seq"), axis=0, tiled=True),
        lax.all_gather(w_value, ("req", "seq"), axis=0, tiled=True),
    )
    query_raw = jnp.dot(flat_rows, full_query, preferred_element_type=jnp.float32)
    key_raw = jnp.dot(flat_rows, full_key, preferred_element_type=jnp.float32)
    value_raw = jnp.dot(flat_rows, full_value, preferred_element_type=jnp.float32)
    local_index = jnp.arange(slice_len, dtype=jnp.int32)
    positions = cache_lengths[:, None] + seq_seat * slice_len + local_index[None, :]
    cosine, sine_part = tables(positions, HEAD)
    queries = (
        rotate(query_raw.reshape(req_local, slice_len, HEADS, HEAD), cosine, sine_part)
        .reshape(req_local, slice_len, HEADS * HEAD)
        .astype(jnp.bfloat16)
    )
    new_keys = (
        rotate(key_raw.reshape(req_local, slice_len, KV_HEADS, HEAD), cosine, sine_part)
        .reshape(req_local, slice_len, KV_HEADS * HEAD)
        .astype(jnp.bfloat16)
    )
    new_values = value_raw.reshape(req_local, slice_len, KV_HEADS * HEAD).astype(jnp.bfloat16)
    all_queries = lax.all_gather(queries, "seq", axis=1, tiled=True)
    key_block = jnp.concatenate([cache_keys, new_keys], axis=1)
    value_block = jnp.concatenate([cache_values, new_values], axis=1)
    span_index = jnp.arange(span_len, dtype=jnp.int32)
    cache_pos = seq_seat * cache_len_dev + jnp.arange(cache_len_dev, dtype=jnp.int32)
    new_pos = seq_seat * slice_len + local_index
    new_live = new_pos[None, :] <= span_index[:, None]
    max_list = []
    sum_list = []
    out_list = []
    for request in range(req_local):
        cache_live = cache_pos < cache_lengths[request]
        live_full = jnp.concatenate(
            [jnp.broadcast_to(cache_live[None, :], (span_len, cache_len_dev)), new_live], axis=1
        )
        query_rows = all_queries[request]
        terms = attend_rows(query_rows, key_block[request], value_block[request], live_full)
        max_list.append(terms[0])
        sum_list.append(terms[1])
        out_list.append(terms[2])
    max_all = jnp.stack(max_list)
    sum_all = jnp.stack(sum_list)
    out_all = jnp.stack(out_list)
    got_max, got_sum = (
        lax.all_to_all(max_all, "seq", split_axis=1, concat_axis=0, tiled=True),
        lax.all_to_all(sum_all, "seq", split_axis=1, concat_axis=0, tiled=True),
    )
    got_out = lax.all_to_all(out_all, "seq", split_axis=1, concat_axis=0, tiled=True)
    got_max = got_max.reshape(seq_count, req_local, slice_len, HEADS)
    got_sum = got_sum.reshape(seq_count, req_local, slice_len, HEADS)
    got_out = got_out.reshape(seq_count, req_local, slice_len, HEADS, HEAD)
    best_max = jnp.max(got_max, axis=0)
    factor = jnp.exp(got_max - best_max)
    total_sum = jnp.sum(got_sum * factor, axis=0)
    total_out = jnp.sum(got_out.astype(jnp.float32) * factor[..., None], axis=0)
    attended = (
        (total_out / total_sum[..., None])
        .reshape(req_local, slice_len, HEADS * HEAD)
        .astype(jnp.bfloat16)
    )
    return (attended, new_keys, new_values)


def solution(mesh):
    in_specs = (
        P("req", "seq", None),
        P(),
        P(("req", "seq"), None),
        P(("req", "seq"), None),
        P(("req", "seq"), None),
        P("req", "seq", None),
        P("req", "seq", None),
        P("req"),
    )
    out_specs = (P("req", "seq", None), P("req", "seq", None), P("req", "seq", None))
    return jax.shard_map(body, mesh=mesh, in_specs=in_specs, out_specs=out_specs, check_vma=False)
```

profile of v0, /device:TPU:32, one launch (start us, length us, event | category | flops | bytes accessed | tf_op | source)
XLA Modules:
  0.0 553.0 jit_solution(8246084704090221894)
XLA Ops:
  11.5 117.5 %all-gather.9.cloned.1.call-done = bf16[2048,1024]{1,0:T(8,128)(2,1)} async-done(((bf16[8,1024]{1,0:T(8,128)(2,1)}), bf16[2048,1024]{1,0:T(8,128)(2,1)}) %all-gather.9.cloned.1.call-update) | async-done | bytes 4194320 | tf_op jit(solution)/shard_map/all_gather | solution.py:89
  129.0 6.6 %copy.99 = bf16[1024,2048]{1,0:T(8,128)(2,1)} copy(bf16[1024,2048]{0,1:T(8,128)(2,1)} %bitcast.163) | data formatting | bytes 8388608 | tf_op jit(solution)/shard_map/dot_general | solution.py:93
  135.6 3.6 fusion.47
  143.7 91.3 %all-gather.7.cloned.1.call-done = bf16[2048,512]{1,0:T(8,128)(2,1)} async-done(((bf16[8,512]{1,0:T(8,128)(2,1)}), bf16[2048,512]{1,0:T(8,128)(2,1)}) %all-gather.7.cloned.1.call-update) | async-done | bytes 2097168 | tf_op jit(solution)/shard_map/all_gather | solution.py:90
  235.0 2.9 copy.97
  239.7 102.3 %all-gather.5.cloned.1.call-done = bf16[2048,512]{1,0:T(8,128)(2,1)} async-done(((bf16[8,512]{1,0:T(8,128)(2,1)}), bf16[2048,512]{1,0:T(8,128)(2,1)}) %all-gather.5.cloned.1.call-update) | async-done | bytes 2097168 | tf_op jit(solution)/shard_map/all_gather | solution.py:91
  342.0 2.1 fusion.40
  346.5 48.8 %all-gather.11.cloned.1.call-done = bf16[2,1024,1024]{2,1,0:T(8,128)(2,1)} async-done(((bf16[2,32,1024]{2,1,0:T(8,128)(2,1)}), bf16[2,1024,1024]{2,1,0:T(8,128)(2,1)}) %all-gather.11.cloned.1.call-update) | async-done | bytes 4194320 | tf_op jit(solution)/shard_map/all_gather | solution.py:110
  395.3 3.9 fusion.87
  399.1 2.3 copy.101
  401.4 3.3 fusion.4
  405.3 3.0 fusion.8
  408.4 3.1 convolution_convert_fusion.3
  412.8 3.4 fusion.5
  416.7 3.9 convolution_convert_fusion.2
  423.1 2.5 fusion.6
  426.9 2.2 fusion.12
  429.1 2.1 convolution_convert_fusion.1
  432.0 2.2 fusion.7
  435.4 3.1 convolution_convert_fusion
  445.7 2.1 reshape.179
  447.8 5.2 all-to-all-start.1
  454.9 3.1 maximum_bitcast_fusion.1
  459.2 3.3 reshape.181
  462.6 7.4 %all-to-all-start.2 = ((f32[32,1,256]{2,1,0:T(1,128)}), f32[32,1,256]{2,1,0:T(1,128)S(1)}, u32[]{:S(2)}, u32[]{:S(2)}) async-start(f32[32,1,256]{2,1,0:T(1,128)} %reshape.181), calls=%async_computation.2 | async-start | bytes 65536 | tf_op jit(solution)/shard_map/all_to_all | solution.py:135
  470.0 2.0 pad_maximum_fusion
  471.9 6.3 %copy.121 = bf16[2,1024,1024]{2,0,1:T(2,128)(2,1)} copy(bf16[2,1024,1024]{2,1,0:T(8,128)(2,1)S(1)} %pad_maximum_fusion) | data formatting | bytes 8388608 | tf_op jit(solution)/shard_map/stack | solution.py:132
  478.2 7.7 %all-to-all-start = ((bf16[2,1024,1024]{2,0,1:T(2,128)(2,1)}), bf16[2,1024,1024]{2,0,1:T(2,128)(2,1)}, u32[]{:S(2)}, u32[]{:S(2)}) async-start(bf16[2,1024,1024]{2,0,1:T(2,128)(2,1)} %copy.121), calls=%async_computation | async-start | bytes 8388608 | tf_op jit(solution)/shard_map/all_to_all | solution.py:137
  493.3 4.5 mul.173
  497.9 10.8 %mul.174 = f32[32,2,32,1024]{3,2,0,1:T(8,128)} reshape(f32[32,2,32,4,256]{4,3,2,0,1:T(4,128)} %mul.173) | data formatting | bytes 16777216 | tf_op jit(solution)/shard_map/mul | solution.py:144
  509.0 30.7 %all-to-all-done = bf16[2,1024,1024]{2,0,1:T(2,128)(2,1)} async-done(((bf16[2,1024,1024]{2,0,1:T(2,128)(2,1)}), bf16[2,1024,1024]{2,0,1:T(2,128)(2,1)}, u32[]{:S(2)}, u32[]{:S(2)}) %all-to-all-start) | async-done | bytes 4194336 | tf_op jit(solution)/shard_map/all_to_all | solution.py:137
  539.7 3.7 copy.122
  (136 shorter events, 42.0 us)
Async XLA Ops:
  7.2 121.8 %all-gather.9.cloned.1.call-start = ((), (), s32[]{:S(2)}) async-start(), calls=%async_computation.5 | async-start | bytes 4210688 | tf_op jit(solution)/shard_map/all_gather | solution.py:89
  7.9 227.1 %all-gather.7.cloned.1.call-start = ((), (), s32[]{:S(2)}) async-start(), calls=%async_computation.4 | async-start | bytes 2105344 | tf_op jit(solution)/shard_map/all_gather | solution.py:90
  8.6 333.3 %all-gather.5.cloned.1.call-start = ((), (), s32[]{:S(2)}) async-start(), calls=%async_computation.3 | async-start | bytes 2105344 | tf_op jit(solution)/shard_map/all_gather | solution.py:91
  9.4 385.9 %all-gather.11.cloned.1.call-start = ((), (), s32[]{:S(2)}) async-start(), calls=%async_computation.6 | async-start | bytes 4325376 | tf_op jit(solution)/shard_map/all_gather | solution.py:110
  129.0 6.6 %copy-start.1 = (bf16[2,32,2048]{2,1,0:T(8,128)(2,1)S(1)}, bf16[2,32,2048]{2,1,0:T(8,128)(2,1)}, u32[]{:S(2)}) copy-start(bf16[2,32,2048]{2,1,0:T(8,128)(2,1)} %param.8) | copy-start | bytes 786436
  129.0 6.6 %copy-start.16 = (f32[2048]{0:T(1024)S(1)}, f32[2048]{0:T(1024)}, u32[]{:S(2)}) copy-start(f32[2048]{0:T(1024)} %param.9) | copy-start | bytes 24580
  135.6 4.4 copy-start.27
  135.6 6.4 %copy-start.10 = (bf16[2,256,512]{2,1,0:T(8,128)(2,1)S(1)}, bf16[2,256,512]{2,1,0:T(8,128)(2,1)}, u32[]{:S(2)}) copy-start(bf16[2,256,512]{2,1,0:T(8,128)(2,1)} %param.13) | copy-start | bytes 1572868
  238.8 105.3 %copy-start.11 = (bf16[2,256,512]{2,1,0:T(8,128)(2,1)S(1)}, bf16[2,256,512]{2,1,0:T(8,128)(2,1)}, u32[]{:S(2)}) copy-start(bf16[2,256,512]{2,1,0:T(8,128)(2,1)} %param.14) | copy-start | bytes 1572868
  344.1 55.0 %copy-start.14 = (bf16[2,32,512]{2,1,0:T(8,128)(2,1)}, bf16[2,32,512]{2,1,0:T(8,128)(2,1)S(1)}, u32[]{:S(2)}) copy-start(bf16[2,32,512]{2,1,0:T(8,128)(2,1)S(1)} %fusion.40) | copy-start | bytes 196612
  405.3 3.0 copy-start.3
  405.3 3.0 copy-start.9
  412.8 4.0 copy-start.13
  416.7 3.9 copy-start.2
  426.9 2.2 copy-start.8
  426.9 2.2 copy-start.12
  426.9 2.2 copy-start.22
  435.4 3.1 copy-start.21
  439.7 2.7 copy-start.6
  441.0 2.7 copy-start.7
  442.4 2.7 copy-start.23
  442.4 2.7 copy-start.24
  442.4 2.7 copy-start.25
  442.4 2.7 copy-start.26
  443.7 9.3 %copy-start.17 = (f32[512,2,2]{0,2,1:T(2,128)S(1)}, f32[512,2,2]{0,2,1:T(2,128)}, u32[]{:S(2)}) copy-start(f32[512,2,2]{0,2,1:T(2,128)} %fusion.8) | copy-start | bytes 24580
  443.7 9.4 %copy-start.18 = (f32[512,2,2]{0,2,1:T(2,128)S(1)}, f32[512,2,2]{0,2,1:T(2,128)}, u32[]{:S(2)}) copy-start(f32[512,2,2]{0,2,1:T(2,128)} %fusion.10) | copy-start | bytes 24580
  443.7 9.4 %copy-start.19 = (f32[512,2,2]{0,2,1:T(2,128)S(1)}, f32[512,2,2]{0,2,1:T(2,128)}, u32[]{:S(2)}) copy-start(f32[512,2,2]{0,2,1:T(2,128)} %fusion.12) | copy-start | bytes 24580
  443.7 9.4 %copy-start.20 = (f32[512,2,2]{0,2,1:T(2,128)S(1)}, f32[512,2,2]{0,2,1:T(2,128)}, u32[]{:S(2)}) copy-start(f32[512,2,2]{0,2,1:T(2,128)} %fusion.14) | copy-start | bytes 24580
  447.8 14.8 %all-to-all-start.1 = ((f32[32,1,256]{2,1,0:T(1,128)}), f32[32,1,256]{2,1,0:T(1,128)S(1)}, u32[]{:S(2)}, u32[]{:S(2)}) async-start(f32[32,1,256]{2,1,0:T(1,128)} %reshape.179), calls=%async_computation.1 | async-start | bytes 65536 | tf_op jit(solution)/shard_map/all_to_all | solution.py:134
  462.6 15.7 %all-to-all-start.2 = ((f32[32,1,256]{2,1,0:T(1,128)}), f32[32,1,256]{2,1,0:T(1,128)S(1)}, u32[]{:S(2)}, u32[]{:S(2)}) async-start(f32[32,1,256]{2,1,0:T(1,128)} %reshape.181), calls=%async_computation.2 | async-start | bytes 65536 | tf_op jit(solution)/shard_map/all_to_all | solution.py:135
  478.2 61.5 %all-to-all-start = ((bf16[2,1024,1024]{2,0,1:T(2,128)(2,1)}), bf16[2,1024,1024]{2,0,1:T(2,128)(2,1)}, u32[]{:S(2)}, u32[]{:S(2)}) async-start(bf16[2,1024,1024]{2,0,1:T(2,128)(2,1)} %copy.121), calls=%async_computation | async-start | bytes 8388608 | tf_op jit(solution)/shard_map/all_to_all | solution.py:137
  539.7 4.6 copy-start
  (3 other events, 3.4 us)
Sparse Core Ops, SparseCore 0:
  11.6 117.4 all-gather.8
  132.7 102.2 all-gather.6
  238.8 103.1 all-gather.4
  345.0 50.2 all-gather.10
where the time goes:
time: 554 us; the launch traced here: 553 us
  waiting for transfers between devices  393 us (71%)
  local copies, waits for them, and re-layouts  73.6 us (13%)
  matrix products  30 us (5%)
  other arithmetic  22 us (4%)
  starting transfers between devices  20.5 us (4%)
  between operations  14.2 us (3%)
    all_gather x1, waiting for transfers between devices, body(): lax.all_gather(w_query, ('req', 'seq'), axis=0, tiled=True)  118 us
    all_gather x1, waiting for transfers between devices, body(): lax.all_gather(w_value, ('req', 'seq'), axis=0, tiled=True)  102 us
    all_gather x1, waiting for transfers between devices, body(): lax.all_gather(w_key, ('req', 'seq'), axis=0, tiled=True)  91.3 us
    all_gather x1, waiting for transfers between devices, body(): all_queries = lax.all_gather(queries, 'seq', axis=1, tiled=True)  48.8 us
    all_to_all x1, waiting for transfers between devices, body(): lax.all_to_all(out_all, 'seq', split_axis=1, concat_axis=0, tiled=True)  30.7 us
    mul x2, local copies, waits for them, and re-layouts, body(): total_out = jnp.sum(got_out.astype(jnp.float32) * factor[..., None], axis=0)  15.3 us
    dot_general x4, matrix products, attend(): jnp.einsum('cgek,kgh->cgeh', weights.astype(jnp.bfloat16), value_view, pr...  12.1 us
    dot_general x4, matrix products, attend(): jnp.einsum('cgeh,kgh->cgek', query_view, key_view, preferred_element_type...  11.4 us
  transfers between devices with their start and end apart: 7, of which 5 were waited for; matrix products, arithmetic and copies ran while one was open for 12% of the time, Pallas kernels for 0%

commit v1 on v0

--- a/solution.py
+++ b/solution.py
@@ -9,6 +9,11 @@
 EPSILON = 1e-06
 THETA = 1000042.0
 MASKED = -1e30
+
+
+def swapped_in(x, axis, dim):
+    sent = jnp.stack([x] * lax.axis_size(axis))
+    return jnp.concatenate(lax.all_to_all(sent, axis, 0, 0), axis=dim)
 
 
 def tables(positions, head_size):
@@ -88,7 +93,7 @@
     full_query, full_key, full_value = (
         lax.all_gather(w_query, ("req", "seq"), axis=0, tiled=True),
         lax.all_gather(w_key, ("req", "seq"), axis=0, tiled=True),
-        lax.all_gather(w_value, ("req", "seq"), axis=0, tiled=True),
+        swapped_in(w_value, ("req", "seq"), 0),
     )
     query_raw = jnp.dot(flat_rows, full_query, preferred_element_type=jnp.float32)
     key_raw = jnp.dot(flat_rows, full_key, preferred_element_type=jnp.float32)

time: 554 us -> 451 us (0.81)
  waiting for transfers between devices: 393 us -> 275 us
  starting transfers between devices: 20.5 us -> 30.7 us
    all_gather x1 -> x0, waiting for transfers between devices: 102 us -> none  [body(): lax.all_gather(w_value, ('req', 'seq'), axis=0, tiled=True)]
    all_to_all x0 -> x1, starting transfers between devices: none -> 10.1 us  [swapped_in(): return jnp.concatenate(lax.all_to_all(sent, axis, 0, 0), axis=dim)]
    all_gather x1, waiting for transfers between devices: 91.3 us -> 83.4 us  [body(): lax.all_gather(w_key, ('req', 'seq'), axis=0, tiled=True)]
    all_gather x1, waiting for transfers between devices: 48.8 us -> 41.6 us  [body(): all_queries = lax.all_gather(queries, 'seq', axis=1, tiled=True)]
  transfers between devices with their start and end apart: 7 -> 7, of which waited for: 5 -> 4; matrix products, arithmetic and copies ran while one was open for 12% -> 16% of each run, Pallas kernels for 0% -> 0%
where the time goes in v1:
time: 451 us; the launch traced here: 450 us
  waiting for transfers between devices  275 us (61%)
  local copies, waits for them, and re-layouts  77 us (17%)
  starting transfers between devices  30.7 us (7%)
  matrix products  30 us (7%)
  other arithmetic  22.8 us (5%)
  between operations  14.2 us (3%)
    all_gather x1, waiting for transfers between devices, body(): lax.all_gather(w_query, ('req', 'seq'), axis=0, tiled=True)  118 us
    all_gather x1, waiting for transfers between devices, body(): lax.all_gather(w_key, ('req', 'seq'), axis=0, tiled=True)  83.4 us
    all_gather x1, waiting for transfers between devices, body(): all_queries = lax.all_gather(queries, 'seq', axis=1, tiled=True)  41.6 us
    all_to_all x1, waiting for transfers between devices, body(): lax.all_to_all(out_all, 'seq', split_axis=1, concat_axis=0, tiled=True)  30.6 us
    mul x2, local copies, waits for them, and re-layouts, body(): total_out = jnp.sum(got_out.astype(jnp.float32) * factor[..., None], axis=0)  15.4 us
    dot_general x4, matrix products, attend(): jnp.einsum('cgek,kgh->cgeh', weights.astype(jnp.bfloat16), value_view, pr...  12.1 us
    dot_general x4, matrix products, attend(): jnp.einsum('cgeh,kgh->cgek', query_view, key_view, preferred_element_type...  11.5 us
    unnamed x67, local copies, waits for them, and re-layouts  10.5 us
  transfers between devices with their start and end apart: 7, of which 4 were waited for; matrix products, arithmetic and copies ran while one was open for 16% of the time, Pallas kernels for 0%

profile of v1, /device:TPU:32, one launch (start us, length us, event | category | flops | bytes accessed | tf_op | source)
XLA Modules:
  0.0 449.9 jit_solution(4956256277310240169)
XLA Ops:
  10.7 118.3 %all-gather.6.cloned.1.call-done = bf16[2048,1024]{1,0:T(8,128)(2,1)} async-done(((bf16[8,1024]{1,0:T(8,128)(2,1)}), bf16[2048,1024]{1,0:T(8,128)(2,1)}) %all-gather.6.cloned.1.call-update) | async-done | bytes 4194320 | tf_op jit(solution)/shard_map/all_gather | solution.py:94
  129.0 6.6 %copy.99 = bf16[1024,2048]{1,0:T(8,128)(2,1)} copy(bf16[1024,2048]{0,1:T(8,128)(2,1)} %bitcast.165) | data formatting | bytes 8388608 | tf_op jit(solution)/shard_map/dot_general | solution.py:98
  135.6 3.6 fusion.47
  141.5 10.1 %all-to-all-start = ((bf16[256,8,512]{2,1,0:T(8,128)(2,1)}), bf16[256,8,512]{2,1,0:T(8,128)(2,1)S(1)}, u32[]{:S(2)}, u32[]{:S(2)}) async-start(bf16[256,8,512]{2,1,0:T(8,128)(2,1)} %stack.20), calls=%async_computation | async-start | bytes 4194304 | tf_op jit(solution)/shard_map/all_to_all | solution.py:16
  155.4 83.4 %all-gather.4.cloned.1.call-done = bf16[2048,512]{1,0:T(8,128)(2,1)} async-done(((bf16[8,512]{1,0:T(8,128)(2,1)}), bf16[2048,512]{1,0:T(8,128)(2,1)}) %all-gather.4.cloned.1.call-update) | async-done | bytes 2097168 | tf_op jit(solution)/shard_map/all_gather | solution.py:95
  238.8 4.0 copy.97
  242.8 2.3 fusion.49
  250.7 41.6 %all-gather.8.cloned.1.call-done = bf16[2,1024,1024]{2,1,0:T(8,128)(2,1)} async-done(((bf16[2,32,1024]{2,1,0:T(8,128)(2,1)}), bf16[2,1024,1024]{2,1,0:T(8,128)(2,1)}) %all-gather.8.cloned.1.call-update) | async-done | bytes 4194320 | tf_op jit(solution)/shard_map/all_gather | solution.py:115
  292.2 3.9 fusion.87
  296.1 2.3 copy.101
  298.4 3.4 fusion.4
  302.4 3.0 fusion.8
  305.4 3.1 convolution_convert_fusion.3
  309.8 3.4 fusion.5
  313.8 3.9 convolution_convert_fusion.2
  320.2 2.5 fusion.6
  324.0 2.0 fusion.12
  326.0 2.1 convolution_convert_fusion.1
  328.9 2.2 fusion.7
  332.4 3.0 convolution_convert_fusion
  342.6 2.1 reshape.185
  344.7 5.3 %all-to-all-start.2 = ((f32[32,1,256]{2,1,0:T(1,128)}), f32[32,1,256]{2,1,0:T(1,128)S(1)}, u32[]{:S(2)}, u32[]{:S(2)}) async-start(f32[32,1,256]{2,1,0:T(1,128)} %reshape.185), calls=%async_computation.2 | async-start | bytes 65536 | tf_op jit(solution)/shard_map/all_to_all | solution.py:139
  351.8 3.0 maximum_bitcast_fusion.1
  356.2 3.3 reshape.187
  359.5 7.6 %all-to-all-start.3 = ((f32[32,1,256]{2,1,0:T(1,128)}), f32[32,1,256]{2,1,0:T(1,128)S(1)}, u32[]{:S(2)}, u32[]{:S(2)}) async-start(f32[32,1,256]{2,1,0:T(1,128)} %reshape.187), calls=%async_computation.3 | async-start | bytes 65536 | tf_op jit(solution)/shard_map/all_to_all | solution.py:140
  367.2 2.0 pad_maximum_fusion
  369.1 6.3 %copy.121 = bf16[2,1024,1024]{2,0,1:T(2,128)(2,1)} copy(bf16[2,1024,1024]{2,1,0:T(8,128)(2,1)S(1)} %pad_maximum_fusion) | data formatting | bytes 8388608 | tf_op jit(solution)/shard_map/stack | solution.py:137
  375.5 7.6 %all-to-all-start.1 = ((bf16[2,1024,1024]{2,0,1:T(2,128)(2,1)}), bf16[2,1024,1024]{2,0,1:T(2,128)(2,1)}, u32[]{:S(2)}, u32[]{:S(2)}) async-start(bf16[2,1024,1024]{2,0,1:T(2,128)(2,1)} %copy.121), calls=%async_computation.1 | async-start | bytes 8388608 | tf_op jit(solution)/shard_map/all_to_all | solution.py:142
  390.4 4.6 %mul.173 = f32[32,2,32,4,256]{4,3,2,0,1:T(4,128)} broadcast(f32[32,2,32,4]{3,2,0,1:T(8,128)S(1)} %copy.125), dimensions={0,1,2,3} | broadcast | bytes 8421376 | tf_op jit(solution)/shard_map/mul | solution.py:149
  394.9 10.8 %mul.174 = f32[32,2,32,1024]{3,2,0,1:T(8,128)} reshape(f32[32,2,32,4,256]{4,3,2,0,1:T(4,128)} %mul.173) | data formatting | bytes 16777216 | tf_op jit(solution)/shard_map/mul | solution.py:149
  406.1 30.6 %all-to-all-done.1 = bf16[2,1024,1024]{2,0,1:T(2,128)(2,1)} async-done(((bf16[2,1024,1024]{2,0,1:T(2,128)(2,1)}), bf16[2,1024,1024]{2,0,1:T(2,128)(2,1)}, u32[]{:S(2)}, u32[]{:S(2)}) %all-to-all-start.1) | async-done | bytes 4194336 | tf_op jit(solution)/shard_map/all_to_all | solution.py:142
  436.7 3.7 copy.122
  (142 shorter events, 44.4 us)
Async XLA Ops:
  7.2 121.8 %all-gather.6.cloned.1.call-start = ((), (), s32[]{:S(2)}) async-start(), calls=%async_computation.5 | async-start | bytes 4210688 | tf_op jit(solution)/shard_map/all_gather | solution.py:94
  7.9 230.9 %all-gather.4.cloned.1.call-start = ((), (), s32[]{:S(2)}) async-start(), calls=%async_computation.4 | async-start | bytes 2105344 | tf_op jit(solution)/shard_map/all_gather | solution.py:95
  8.6 283.6 %all-gather.8.cloned.1.call-start = ((), (), s32[]{:S(2)}) async-start(), calls=%async_computation.6 | async-start | bytes 4325376 | tf_op jit(solution)/shard_map/all_gather | solution.py:115
  129.0 6.6 %copy-start.1 = (bf16[2,32,2048]{2,1,0:T(8,128)(2,1)S(1)}, bf16[2,32,2048]{2,1,0:T(8,128)(2,1)}, u32[]{:S(2)}) copy-start(bf16[2,32,2048]{2,1,0:T(8,128)(2,1)} %param.8) | copy-start | bytes 786436
  129.0 6.6 %copy-start.18 = (f32[2048]{0:T(1024)S(1)}, f32[2048]{0:T(1024)}, u32[]{:S(2)}) copy-start(f32[2048]{0:T(1024)} %param.9) | copy-start | bytes 24580
  135.6 4.4 copy-start.29
  141.5 10.1 %copy-start.30 = (s32[2]{0:T(128)S(1)}, s32[2]{0:T(128)}, u32[]{:S(2)}) copy-start(s32[2]{0:T(128)} %param.15) | copy-start | bytes 28
  141.5 12.1 %copy-start.13 = (bf16[2,256,512]{2,1,0:T(8,128)(2,1)S(1)}, bf16[2,256,512]{2,1,0:T(8,128)(2,1)}, u32[]{:S(2)}) copy-start(bf16[2,256,512]{2,1,0:T(8,128)(2,1)} %param.13) | copy-start | bytes 1572868
  141.5 105.2 %all-to-all-start = ((bf16[256,8,512]{2,1,0:T(8,128)(2,1)}), bf16[256,8,512]{2,1,0:T(8,128)(2,1)S(1)}, u32[]{:S(2)}, u32[]{:S(2)}) async-start(bf16[256,8,512]{2,1,0:T(8,128)(2,1)} %stack.20), calls=%async_computation | async-start | bytes 4194304 | tf_op jit(solution)/shard_map/all_to_all | solution.py:16
  247.2 3.5 copy-start.16
  250.7 47.7 %copy-start.12 = (pred[512,288]{0,1:T(8,128)(4,1)S(1)}, pred[512,288]{0,1:T(8,128)(4,1)}, u32[]{:S(2)}) copy-start(pred[512,288]{0,1:T(8,128)(4,1)} %get-tuple-element.13) | copy-start | bytes 442372
  302.4 3.0 copy-start.3
  305.4 4.4 copy-start.11
  309.8 4.0 copy-start.15
  313.8 3.9 copy-start.2
  317.7 2.5 copy-start.9
  326.0 2.9 copy-start.8
  332.4 3.0 copy-start.23
  336.6 2.7 copy-start.6
  337.9 2.7 copy-start.7
  339.3 2.7 copy-start.25
  339.3 2.7 copy-start.26
  339.3 2.7 copy-start.27
  339.3 2.7 copy-start.28
  340.6 9.4 %copy-start.19 = (f32[512,2,2]{0,2,1:T(2,128)S(1)}, f32[512,2,2]{0,2,1:T(2,128)}, u32[]{:S(2)}) copy-start(f32[512,2,2]{0,2,1:T(2,128)} %fusion.8) | copy-start | bytes 24580
  340.6 9.4 %copy-start.20 = (f32[512,2,2]{0,2,1:T(2,128)S(1)}, f32[512,2,2]{0,2,1:T(2,128)}, u32[]{:S(2)}) copy-start(f32[512,2,2]{0,2,1:T(2,128)} %fusion.10) | copy-start | bytes 24580
  340.6 9.4 %copy-start.21 = (f32[512,2,2]{0,2,1:T(2,128)S(1)}, f32[512,2,2]{0,2,1:T(2,128)}, u32[]{:S(2)}) copy-start(f32[512,2,2]{0,2,1:T(2,128)} %fusion.12) | copy-start | bytes 24580
  340.6 9.4 %copy-start.22 = (f32[512,2,2]{0,2,1:T(2,128)S(1)}, f32[512,2,2]{0,2,1:T(2,128)}, u32[]{:S(2)}) copy-start(f32[512,2,2]{0,2,1:T(2,128)} %fusion.14) | copy-start | bytes 24580
  344.7 14.8 %all-to-all-start.2 = ((f32[32,1,256]{2,1,0:T(1,128)}), f32[32,1,256]{2,1,0:T(1,128)S(1)}, u32[]{:S(2)}, u32[]{:S(2)}) async-start(f32[32,1,256]{2,1,0:T(1,128)} %reshape.185), calls=%async_computation.2 | async-start | bytes 65536 | tf_op jit(solution)/shard_map/all_to_all | solution.py:139
  359.5 15.9 %all-to-all-start.3 = ((f32[32,1,256]{2,1,0:T(1,128)}), f32[32,1,256]{2,1,0:T(1,128)S(1)}, u32[]{:S(2)}, u32[]{:S(2)}) async-start(f32[32,1,256]{2,1,0:T(1,128)} %reshape.187), calls=%async_computation.3 | async-start | bytes 65536 | tf_op jit(solution)/shard_map/all_to_all | solution.py:140
  375.5 61.2 %all-to-all-start.1 = ((bf16[2,1024,1024]{2,0,1:T(2,128)(2,1)}), bf16[2,1024,1024]{2,0,1:T(2,128)(2,1)}, u32[]{:S(2)}, u32[]{:S(2)}) async-start(bf16[2,1024,1024]{2,0,1:T(2,128)(2,1)} %copy.121), calls=%async_computation.1 | async-start | bytes 8388608 | tf_op jit(solution)/shard_map/all_to_all | solution.py:142
  436.7 4.6 %copy-start = (f32[32,2,32,1024]{3,2,0,1:T(8,128)S(1)}, f32[32,2,32,1024]{3,2,0,1:T(8,128)}, u32[]{:S(2)}) copy-start(f32[32,2,32,1024]{3,2,0,1:T(8,128)} %mul.174) | copy-start | bytes 25165828
  (6 other events, 9.1 us)
Sparse Core Ops, SparseCore 0:
  11.6 117.4 all-gather.5
  132.7 106.0 all-gather.3
  242.0 50.2 all-gather.7
